TPU v7x, 32 devices: a whole 2x2x4 slice. The times are simulated.
32 devices in a mesh: dp: 4 (over z), expert: 4 (over y, core), etp: 2 (over x).
Axes of the slice: x: 2, y: 2, z: 4, core: 2. Of those that a mesh axis runs over, the one named last changes fastest.
Arguments:
- grad_out: bfloat16 [2048, 4096], P(('dp', 'expert')), may hold values from -3 to 3
- routes: int32 [2048, 8], P(('dp', 'expert')), may hold values from 0 to 15, all different within a row; in each aligned block of 128 rows (0 to 127, 128 to 255, ...) at most 80 rows name the same one
- gates: bfloat16 [2048, 8], P(('dp', 'expert')), may hold values from 0.099609375 to 1
- hidden_saved: bfloat16 [4, 16, 320, 1536], P('dp', 'expert', None, 'etp'), may hold values from -1.5 to 1.5
- down_weight: bfloat16 [16, 1536, 4096], P('expert', 'etp', 'dp'), may hold values from -0.15625 to 0.15625
Outputs:
- weight_grad: bfloat16 [16, 1536, 4096], P('expert', 'etp', 'dp')
- hidden_grad: bfloat16 [4, 16, 320, 1536], P('dp', 'expert', None, 'etp')
- gate_grad: float32 [2048, 8], P(('dp', 'expert'))
Inputs may be any that keep to these rules, and one draw needn't show every extreme that they name: `routes`: each row names 8 different experts. Within the rows of one device (aligned blocks of 128 rows) no expert is named more than 80 times, a bound that some block reaches.
All inputs are finite; a program needn't handle non-finite values.
Results may differ from a plain program's by a relative error of at most 0.005.
Values may be sent and summed in bfloat16 or wider, within the bound.
No kernel may reach another device: no remote copies, remote signals or barrier semaphores. Data moves between devices by JAX's collectives and lax.ppermute only.
A program may use at most 192 MiB of HBM per device.

v0:
```python
import jax
import jax.numpy as jnp
from jax import lax
from jax.sharding import PartitionSpec as P


def body(grad_out, routes, gates, hidden_saved, down_weight):
    token_count = grad_out.shape[0]
    top_count = routes.shape[1]
    exp_dev, ff_part, quarter = down_weight.shape
    groups = lax.axis_size("dp")
    senders = lax.axis_size("expert")
    slot_rows_all = hidden_saved.shape[2]
    capacity = slot_rows_all // senders
    experts = exp_dev * senders
    columns = lax.all_to_all(grad_out, "dp", split_axis=1, concat_axis=0, tiled=True)
    all_routes, all_gates = (
        lax.all_gather(routes, "dp", axis=0, tiled=True),
        lax.all_gather(gates, "dp", axis=0, tiled=True),
    )
    pair_routes = all_routes.reshape(groups, token_count * top_count)
    expert_ids = jnp.arange(experts, dtype=jnp.int32)
    onehot = (pair_routes[:, :, None] == expert_ids[None, None, :]).astype(jnp.int32)
    before = jnp.cumsum(onehot, axis=1) - onehot
    slot_ids = jnp.sum(before * onehot, axis=2)
    group_ids = jnp.arange(groups, dtype=jnp.int32)[:, None]
    position = ((group_ids * experts + pair_routes) * capacity + slot_ids).reshape(-1)
    source_rows = (
        group_ids * token_count
        + jnp.arange(token_count * top_count, dtype=jnp.int32)[None, :] // top_count
    ).reshape(-1)
    row_table = (
        jnp.zeros((groups * experts * capacity,), jnp.int32).at[position].set(source_rows + 1)
    )
    gate_table = (
        jnp.zeros((groups * experts * capacity,), gates.dtype)
        .at[position]
        .set(all_gates.reshape(-1))
    )
    row_table = (
        row_table.reshape(groups, senders, exp_dev, capacity).transpose(2, 0, 1, 3).reshape(-1)
    )
    gate_table = gate_table.reshape(groups, senders, exp_dev, capacity).transpose(2, 0, 1, 3)
    filled = row_table > 0
    safe_rows = jnp.maximum(row_table - 1, 0)
    picked = jnp.where(filled[:, None], columns[safe_rows], jnp.zeros((1, quarter), columns.dtype))
    picked = picked.reshape(exp_dev, groups, senders, capacity, quarter)
    received, got_gates = (
        lax.all_to_all(picked, "expert", split_axis=2, concat_axis=2, tiled=True),
        lax.all_to_all(gate_table, "expert", split_axis=2, concat_axis=2, tiled=True),
    )
    received = received.reshape(exp_dev, groups, slot_rows_all, quarter)
    got_gates = got_gates.reshape(exp_dev, groups, slot_rows_all)
    slot_rows = received
    slot_gates = got_gates.astype(jnp.float32)
    scaled = (
        jnp.moveaxis(slot_gates, 0, 1)[..., None]
        * lax.all_gather(hidden_saved, "dp", axis=0, tiled=True).astype(jnp.float32)
    ).astype(jnp.bfloat16)
    weight_sum = jnp.einsum("nerf,enrd->efd", scaled, slot_rows, preferred_element_type=jnp.float32)
    weight_grad = weight_sum.astype(jnp.bfloat16)
    slot_rows = received
    expert_grad = lax.psum_scatter(
        jnp.einsum("enrd,efd->nerf", slot_rows, down_weight, preferred_element_type=jnp.float32),
        "dp",
        scatter_dimension=0,
        tiled=True,
    )
    own_gates = jnp.moveaxis(
        lax.dynamic_slice_in_dim(got_gates, lax.axis_index("dp"), 1, 1), 0, 1
    ).astype(jnp.float32)
    hidden_grad = (own_gates[..., None] * expert_grad).astype(jnp.bfloat16)
    slot_dots = jnp.sum(hidden_saved.astype(jnp.float32) * expert_grad, axis=3)
    slot_dots = slot_dots.reshape(exp_dev, senders, capacity)
    slot_dots = lax.psum(slot_dots, "etp")
    returned = lax.all_to_all(slot_dots, "expert", split_axis=1, concat_axis=1, tiled=True)
    own_slots = lax.dynamic_slice_in_dim(slot_ids, lax.axis_index("dp"), 1, 0).reshape(
        token_count, top_count
    )
    lookup = (routes % exp_dev * senders + routes // exp_dev) * capacity + own_slots
    gate_grad = returned.reshape(-1)[lookup]
    return (weight_grad, hidden_grad, gate_grad)


def solution(mesh):
    in_specs = (
        P(("dp", "expert"), None),
        P(("dp", "expert"), None),
        P(("dp", "expert"), None),
        P("dp", "expert", None, "etp"),
        P("expert", "etp", "dp"),
    )
    out_specs = (
        P("expert", "etp", "dp"),
        P("dp", "expert", None, "etp"),
        P(("dp", "expert"), None),
    )
    return jax.shard_map(body, mesh=mesh, in_specs=in_specs, out_specs=out_specs, check_vma=False)
```

profile of v0, /device:TPU:0, one launch (start us, length us, event | category | flops | bytes accessed | tf_op | source)
XLA Modules:
  0.0 954.9 jit_solution(11956927413460439206)
XLA Ops:
  7.2 2.3 copy.112
  9.4 6.3 all-to-all-start.1
  15.8 0.0 all-reduce.3.cloned.1.call-start
  15.8 31.1 %all_gather.9 = s32[512,8]{0,1:T(8,128)S(1)} all-gather(s32[128,8]{0,1:T(8,128)} %param.6), channel_id=1, replica_groups=mesh['dp'=4,'expert'=4,'etp'=2] {'dp'}, dimensions={0}, use_global_device_ids=true | all-gather | bytes 20480 | tf_op jit(solution)/shard_map/all_gather | solution.py:18
  46.9 0.1 copy.70
  47.0 0.2 eq.31
  47.2 0.2 eq.27
  47.4 0.2 reshape.195
  47.5 0.1 add_bitcast_fusion
  47.6 0.1 broadcast_bitcast_fusion
  47.7 18.0 %reduce-window.6 = s32[4,16,8,128]{3,2,1,0:T(8,128)S(1)} reduce-window(s32[4,16,8,128]{3,2,1,0:T(8,128)S(1)} %fusion.11, s32[]{:T(128)} %constant.65.clone.1), window={size=1x1x1x128 pad=0_0x0_0x0_0x127_0}, to_apply=%region_0.0 | reduce-window | flops 8323072 | bytes 524292 | tf_op jit(solution)/shard_map/reduce-window
  65.7 0.1 slice.12
  65.9 0.3 copy.73
  66.2 0.1 copy.74
  66.3 0.1 broadcast_add_fusion
  66.5 0.1 fusion.10
  66.6 15.5 %scatter_custom_fusion.1 = s32[5120]{0:T(1024)S(1)} fusion(s32[4096]{0:T(1024)S(1)} %bitcast.80, s32[4096]{0:T(1024)S(1)} %bitcast.79, s32[]{:T(128)} %constant.65.clone.1), kind=kCustom, calls=%fused_computation.46 | custom fusion | bytes 20484 | tf_op jit(solution)/shard_map/scatter | solution.py:33
  82.2 0.1 gt.14
  82.3 0.1 max.20
  82.4 0.1 reshape.207
  82.5 0.0 all-to-all-done.1
  82.5 22.6 %gather_fusion = bf16[5120,1024]{1,0:T(8,128)(2,1)} fusion(bf16[512,1024]{1,0:T(8,128)(2,1)S(1)} %bitcast.67, s32[5120]{0:T(1024)S(1)} %broadcast_clamp_fusion), kind=kCustom, calls=%fused_computation | custom fusion | bytes 20992000 | tf_op jit(solution)/shard_map/gather | solution.py:46
  105.1 6.3 copy_select_fusion
  111.4 119.5 %all_to_all.34 = bf16[4,4,4,80,1024]{4,3,0,1,2:T(8,128)(2,1)} all-to-all(bf16[4,4,4,80,1024]{4,3,0,1,2:T(8,128)(2,1)S(1)} %copy_select_fusion), channel_id=1, replica_groups=mesh['dp'=4,'expert'=4,'etp'=2] {'expert'}, dimensions={2} | all-to-all | bytes 20971520 | tf_op jit(solution)/shard_map/all_to_all | solution.py:49
  230.9 10.1 %copy.83 = bf16[4,4,4,80,1024]{4,3,2,0,1:T(8,128)(2,1)} copy(bf16[4,4,4,80,1024]{4,3,0,1,2:T(8,128)(2,1)} %all_to_all.34) | data formatting | bytes 20971520 | tf_op jit(solution)/shard_map/all_to_all | solution.py:49
  241.0 16.0 %fusion.2 = f32[4,4,320,768]{3,2,0,1:T(8,128)} fusion(bf16[4,4,320,1024]{3,2,0,1:T(8,128)(2,1)} %bitcast.69, bf16[4,768,1024]{2,1,0:T(8,128)(2,1)} %param.9), kind=kOutput, calls=%fused_computation.9 | convolution fusion | flops 8053063680 | bytes 32505856 | tf_op jit(solution)/shard_map/enrd,efd->nerf/dot_general | solution.py:64
  257.1 0.0 copy-start.2
  257.1 0.0 copy-start.1
  257.1 0.0 copy-start.3
  257.1 0.0 copy-start
  257.1 0.0 all-reduce.3.cloned.1.call-update
  257.1 0.0 all-gather.2.cloned.1.call-start
  257.2 0.7 all-gather.2.cloned.1.call-update
  257.9 0.0 copy-done.2
  257.9 12.1 %all_gather.10 = bf16[512,8]{0,1:T(8,128)(2,1)S(1)} all-gather(bf16[128,8]{0,1:T(8,128)(2,1)S(1)} %copy-done.2), channel_id=1, replica_groups=mesh['dp'=4,'expert'=4,'etp'=2] {'dp'}, dimensions={0}, use_global_device_ids=true | all-gather | bytes 10240 | tf_op jit(solution)/shard_map/all_gather | solution.py:19
  270.0 0.2 copy.75
  270.2 0.2 reshape.225
  270.3 28.6 %scatter_custom_fusion = bf16[5120]{0:T(1024)(128)(2,1)S(1)} fusion(s32[4096]{0:T(1024)S(1)} %bitcast.81, bf16[4096]{0:T(1024)(128)(2,1)S(1)} %reshape.225, bf16[]{:T(256)} %constant.62.clone.1), kind=kCustom, calls=%fused_computation.55 | custom fusion | bytes 10242 | tf_op jit(solution)/shard_map/scatter | solution.py:38
  298.9 0.1 reshape.198
  299.0 0.6 copy.76
  299.6 3.3 all-to-all-start
  302.9 0.0 copy-done.1
  302.9 0.1 copy.88
  303.0 0.1 reshape.203
  303.1 0.1 compare_select_fusion
  303.2 0.1 reshape.215
  303.3 0.0 copy-done.3
  303.3 0.6 dynamic-slice
  303.9 2.8 all-to-all-done
  306.7 0.1 reshape.199
  306.9 477.1 %all-reduce.3.cloned.1.call-done = f32[4,4,320,768]{3,2,0,1:T(8,128)} async-done(((f32[4,4,320,768]{3,2,0,1:T(8,128)}), f32[4,4,320,768]{3,2,0,1:T(8,128)}) %all-reduce.3.cloned.1.call-update) | async-done | bytes 15728656
  784.0 0.0 copy-done
  784.0 4.7 multiply_reduce_fusion
  788.7 0.1 reshape.201
  788.8 5.0 psum.7
  793.8 0.6 copy.86
  794.4 3.2 all-to-all-start.3
  797.6 127.9 %all-gather.2.cloned.1.call-done = bf16[4,4,320,768]{3,2,1,0:T(8,128)(2,1)} async-done(((bf16[1,4,320,768]{3,2,1,0:T(8,128)(2,1)}), bf16[4,4,320,768]{3,2,1,0:T(8,128)(2,1)}) %all-gather.2.cloned.1.call-update) | async-done | bytes 7864336 | tf_op jit(solution)/shard_map/all_gather | solution.py:58
  925.5 15.5 %bitcast_convert_fusion = bf16[4,768,1024]{2,1,0:T(8,128)(2,1)} fusion(bf16[4,4,320,1024]{3,2,0,1:T(8,128)(2,1)} %bitcast.70, bf16[4,4,320,768]{3,2,1,0:T(8,128)(2,1)} %all-gather.2.cloned.1.call-done, f32[4,4,320]{2,1,0:T(4,128)S(1)} %copy.78), kind=kOutput, calls=%fused_computation.5 | convolution fusion | flops 8068005888 | bytes 24662016 | tf_op jit(solution)/shard_map/nerf,enrd->efd/dot_general | solution.py:60
  941.0 0.0 all-to-all-done.3
  941.0 0.1 reshape.202
  941.1 6.2 gather_fusion.1
  947.3 0.1 reshape.214
  947.4 0.7 copy.93
  (23 shorter events, 0.3 us)
Async XLA Ops:
  9.4 73.1 %all-to-all-start.1 = ((bf16[128,4,1024]{2,0,1:T(8,128)(2,1)}), bf16[128,4,1024]{2,0,1:T(8,128)(2,1)S(1)}, u32[]{:S(2)}, u32[]{:S(2)}) async-start(bf16[128,4,1024]{2,0,1:T(8,128)(2,1)} %bitcast.62), calls=%async_computation.1 | async-start | bytes 2097152 | tf_op jit(solution)/shard_map/all_to_all | solution.py:16
  15.8 768.2 %all-reduce.3.cloned.1.call-start = ((), (), s32[]{:S(2)}) async-start(), calls=%async_computation.5 | async-start | bytes 31457280
  257.1 0.8 copy-start.2
  257.1 45.8 %copy-start.1 = (s32[128,8]{0,1:T(8,128)S(1)}, s32[128,8]{0,1:T(8,128)}, u32[]{:S(2)}) copy-start(s32[128,8]{0,1:T(8,128)} %param.6) | copy-start | bytes 12292
  257.1 46.2 %copy-start.3 = (u32[32]{0:T(128)S(1)}, u32[32]{0:T(128)}, u32[]{:S(2)}) copy-start(u32[32]{0:T(128)} %constant.80) | copy-start | bytes 388
  257.1 526.9 %copy-start = (bf16[1,4,320,768]{3,2,1,0:T(8,128)(2,1)S(1)}, bf16[1,4,320,768]{3,2,1,0:T(8,128)(2,1)}, u32[]{:S(2)}) copy-start(bf16[1,4,320,768]{3,2,1,0:T(8,128)(2,1)} %param.8) | copy-start | bytes 5898244
  257.1 668.4 %all-gather.2.cloned.1.call-start = ((), (), s32[]{:S(2)}) async-start(), calls=%async_computation.4 | async-start | bytes 9830400 | tf_op jit(solution)/shard_map/all_gather | solution.py:58
  299.6 7.1 all-to-all-start
  794.4 146.7 %all-to-all-start.3 = ((f32[4,4,80]{2,0,1:T(4,128)}), f32[4,4,80]{2,0,1:T(4,128)S(1)}, u32[]{:S(2)}, u32[]{:S(2)}) async-start(f32[4,4,80]{2,0,1:T(4,128)} %copy.86), calls=%async_computation.3 | async-start | bytes 16384 | tf_op jit(solution)/shard_map/all_to_all | solution.py:76
Sparse Core Ops, SparseCore 0:
  257.2 526.7 all-reduce.2
  785.6 139.8 all-gather.1
where the time goes:
time: 955 us
  waiting for transfers between devices  609 us (64%)
  blocking collectives  168 us (18%)
  local copies, waits for them, and re-layouts  90.3 us (9%)
  matrix products  31.6 us (3%)
  other arithmetic  29.6 us (3%)
  between operations  14.4 us (2%)
  starting transfers between devices  12.9 us (1%)
    unnamed x3, waiting for transfers between devices  478 us
    all_gather x1, waiting for transfers between devices, body(): lax.all_gather(hidden_saved, 'dp', axis=0, tiled=True).astype(jnp.float32)  128 us
    all_to_all x1, blocking collectives, body(): lax.all_to_all(picked, 'expert', split_axis=2, concat_axis=2, tiled=True)  120 us
    all_gather x1, blocking collectives, body(): lax.all_gather(routes, 'dp', axis=0, tiled=True)  31.1 us
    scatter x1, local copies, waits for them, and re-layouts, body(): gate_table = jnp.zeros((groups * experts * capacity,), gates.dtype).at[po...  28.6 us
    gather x1, local copies, waits for them, and re-layouts, body(): columns[safe_rows]  22.6 us
  transfers between devices with their start and end apart: 5, of which 3 were waited for; matrix products, arithmetic and copies ran while one was open for 9% of the time, Pallas kernels for 0%

commit v1 on v0

--- a/solution.py
+++ b/solution.py
@@ -2,6 +2,18 @@
 import jax.numpy as jnp
 from jax import lax
 from jax.sharding import PartitionSpec as P
+
+
+def gather_by_bits(x, axis, dim):
+    ways, here = (lax.axis_size(axis), lax.axis_index(axis))
+    grown, reach = (x, 1)
+    while reach < ways:
+        theirs = lax.ppermute(grown, axis, [(d, d ^ reach) for d in range(ways)])
+        mine_first = jnp.concatenate([grown, theirs], axis=dim)
+        theirs_first = jnp.concatenate([theirs, grown], axis=dim)
+        grown = jnp.where(here & reach == 0, mine_first, theirs_first)
+        reach = 2 * reach
+    return grown
 
 
 def body(grad_out, routes, gates, hidden_saved, down_weight):
@@ -55,7 +67,7 @@
     slot_gates = got_gates.astype(jnp.float32)
     scaled = (
         jnp.moveaxis(slot_gates, 0, 1)[..., None]
-        * lax.all_gather(hidden_saved, "dp", axis=0, tiled=True).astype(jnp.float32)
+        * gather_by_bits(hidden_saved, "dp", 0).astype(jnp.float32)
     ).astype(jnp.bfloat16)
     weight_sum = jnp.einsum("nerf,enrd->efd", scaled, slot_rows, preferred_element_type=jnp.float32)
     weight_grad = weight_sum.astype(jnp.bfloat16)

time: 955 us -> 1010 us (1.058)
  blocking collectives: 168 us -> 493 us
  waiting for transfers between devices: 609 us -> 333 us
    all_gather x1, blocking collectives: 12.1 us -> 338 us  [body(): lax.all_gather(gates, 'dp', axis=0, tiled=True)]
    unnamed x3 -> x2, waiting for transfers between devices: 478 us -> 188 us
    ppermute x0 -> x2, waiting for transfers between devices: none -> 142 us  [gather_by_bits(): theirs = lax.ppermute(grown, axis, [(d, d ^ reach) for d in range(ways)])]
    all_gather x1 -> x0, waiting for transfers between devices: 128 us -> none  [body(): lax.all_gather(hidden_saved, 'dp', axis=0, tiled=True).astype(jnp.float32)]
  transfers between devices with their start and end apart: 5 -> 6, of which waited for: 3 -> 3; matrix products, arithmetic and copies ran while one was open for 9% -> 9% of each run, Pallas kernels for 0% -> 0%
where the time goes in v1:
time: 1010 us
  blocking collectives  493 us (49%)
  waiting for transfers between devices  333 us (33%)
  local copies, waits for them, and re-layouts  91.8 us (9%)
  other arithmetic  33.8 us (3%)
  matrix products  31.5 us (3%)
  between operations  14.3 us (1%)
  starting transfers between devices  13.8 us (1%)
    all_gather x1, blocking collectives, body(): lax.all_gather(gates, 'dp', axis=0, tiled=True)  338 us
    unnamed x2, waiting for transfers between devices  188 us
    ppermute x2, waiting for transfers between devices, gather_by_bits(): theirs = lax.ppermute(grown, axis, [(d, d ^ reach) for d in range(ways)])  142 us
    all_to_all x1, blocking collectives, body(): lax.all_to_all(picked, 'expert', split_axis=2, concat_axis=2, tiled=True)  120 us
    all_gather x1, blocking collectives, body(): lax.all_gather(routes, 'dp', axis=0, tiled=True)  31.1 us
    scatter x1, local copies, waits for them, and re-layouts, body(): gate_table = jnp.zeros((groups * experts * capacity,), gates.dtype).at[po...  28.6 us
    gather x1, local copies, waits for them, and re-layouts, body(): columns[safe_rows]  22.6 us
  transfers between devices with their start and end apart: 6, of which 3 were waited for; matrix products, arithmetic and copies ran while one was open for 9% of the time, Pallas kernels for 0%

profile of v1, /device:TPU:0, one launch (start us, length us, event | category | flops | bytes accessed | tf_op | source)
XLA Modules:
  0.0 1011.8 jit_solution(13430955871021758867)
XLA Ops:
  7.2 2.3 copy.112
  9.4 6.3 all-to-all-start.1
  15.8 0.0 all-reduce.3.cloned.1.call-start
  15.8 31.1 %all_gather.6 = s32[512,8]{0,1:T(8,128)S(1)} all-gather(s32[128,8]{0,1:T(8,128)} %param.6), channel_id=1, replica_groups=mesh['dp'=4,'expert'=4,'etp'=2] {'dp'}, dimensions={0}, use_global_device_ids=true | all-gather | bytes 20480 | tf_op jit(solution)/shard_map/all_gather | solution.py:30
  46.9 0.1 copy.70
  47.0 0.2 eq.37
  47.2 0.2 eq.33
  47.4 0.2 reshape.195
  47.5 0.1 add_bitcast_fusion
  47.6 0.1 broadcast_bitcast_fusion
  47.7 18.0 %reduce-window.6 = s32[4,16,8,128]{3,2,1,0:T(8,128)S(1)} reduce-window(s32[4,16,8,128]{3,2,1,0:T(8,128)S(1)} %fusion.17, s32[]{:T(128)} %constant.67.clone.1), window={size=1x1x1x128 pad=0_0x0_0x0_0x127_0}, to_apply=%region_0.0 | reduce-window | flops 8323072 | bytes 524292 | tf_op jit(solution)/shard_map/reduce-window
  65.7 0.1 slice.12
  65.9 0.3 copy.73
  66.2 0.1 copy.74
  66.3 0.1 broadcast_add_fusion
  66.5 0.1 fusion.16
  66.6 15.5 %scatter_custom_fusion.1 = s32[5120]{0:T(1024)S(1)} fusion(s32[4096]{0:T(1024)S(1)} %bitcast.80, s32[4096]{0:T(1024)S(1)} %bitcast.79, s32[]{:T(128)} %constant.67.clone.1), kind=kCustom, calls=%fused_computation.54 | custom fusion | bytes 20484 | tf_op jit(solution)/shard_map/scatter | solution.py:45
  82.2 0.1 gt.14
  82.3 0.1 max.20
  82.4 0.1 reshape.207
  82.5 0.0 all-to-all-done.1
  82.5 22.6 %gather_fusion = bf16[5120,1024]{1,0:T(8,128)(2,1)} fusion(bf16[512,1024]{1,0:T(8,128)(2,1)S(1)} %bitcast.67, s32[5120]{0:T(1024)S(1)} %broadcast_clamp_fusion), kind=kCustom, calls=%fused_computation | custom fusion | bytes 20992000 | tf_op jit(solution)/shard_map/gather | solution.py:58
  105.1 6.3 copy_select_fusion
  111.4 119.5 %all_to_all.34 = bf16[4,4,4,80,1024]{4,3,0,1,2:T(8,128)(2,1)} all-to-all(bf16[4,4,4,80,1024]{4,3,0,1,2:T(8,128)(2,1)S(1)} %copy_select_fusion), channel_id=1, replica_groups=mesh['dp'=4,'expert'=4,'etp'=2] {'expert'}, dimensions={2} | all-to-all | bytes 20971520 | tf_op jit(solution)/shard_map/all_to_all | solution.py:61
  230.9 10.1 copy.83
  241.0 16.0 %fusion.2 = f32[4,4,320,768]{3,2,0,1:T(8,128)} fusion(bf16[4,4,320,1024]{3,2,0,1:T(8,128)(2,1)} %bitcast.69, bf16[4,768,1024]{2,1,0:T(8,128)(2,1)} %param.9), kind=kOutput, calls=%fused_computation.9 | convolution fusion | flops 8053063680 | bytes 32505856 | tf_op jit(solution)/shard_map/enrd,efd->nerf/dot_general | solution.py:76
  257.1 0.0 copy-start
  257.1 0.0 all-reduce.3.cloned.1.call-update
  257.1 1.5 copy-done
  258.6 0.0 copy-start.2
  258.6 0.6 collective-permute-start
  259.2 142.2 %collective-permute-done = bf16[1,4,320,768]{3,2,1,0:T(8,128)(2,1)} collective-permute-done((bf16[1,4,320,768]{3,2,1,0:T(8,128)(2,1)S(1)}, bf16[1,4,320,768]{3,2,1,0:T(8,128)(2,1)}, u32[]{:S(2)}, u32[]{:S(2)}) %collective-permute-start) | collective-permute-done | bytes 1966112 | tf_op jit(solution)/shard_map/ppermute | solution.py:11
  401.4 4.3 maximum_select_fusion.2
  405.7 0.4 collective-permute-start.1
  406.1 0.0 copy-done.2
  406.1 337.7 %all_gather.7 = bf16[512,8]{0,1:T(8,128)(2,1)S(1)} all-gather(bf16[128,8]{0,1:T(8,128)(2,1)S(1)} %copy-done.2), channel_id=1, replica_groups=mesh['dp'=4,'expert'=4,'etp'=2] {'dp'}, dimensions={0}, use_global_device_ids=true | all-gather | bytes 10240 | tf_op jit(solution)/shard_map/all_gather | solution.py:31
  743.8 0.2 copy.75
  743.9 0.2 reshape.225
  744.1 28.6 %scatter_custom_fusion = bf16[5120]{0:T(1024)(128)(2,1)S(1)} fusion(s32[4096]{0:T(1024)S(1)} %bitcast.81, bf16[4096]{0:T(1024)(128)(2,1)S(1)} %reshape.225, bf16[]{:T(256)} %constant.64.clone.1), kind=kCustom, calls=%fused_computation.63 | custom fusion | bytes 10242 | tf_op jit(solution)/shard_map/scatter | solution.py:50
  772.7 0.1 reshape.198
  772.8 0.6 copy.76
  773.4 3.3 all-to-all-start
  776.6 0.0 copy-done.1
  776.7 0.1 copy.88
  776.8 0.1 reshape.203
  776.9 0.1 compare_select_fusion
  777.0 0.1 reshape.215
  777.1 0.0 copy-done.3
  777.1 0.6 dynamic-slice
  777.7 2.8 all-to-all-done
  780.5 0.1 reshape.199
  780.6 188.2 %all-reduce.3.cloned.1.call-done = f32[4,4,320,768]{3,2,0,1:T(8,128)} async-done(((f32[4,4,320,768]{3,2,0,1:T(8,128)}), f32[4,4,320,768]{3,2,0,1:T(8,128)}) %all-reduce.3.cloned.1.call-update) | async-done | bytes 15728656
  968.9 4.7 multiply_reduce_fusion
  973.6 0.1 reshape.201
  973.7 5.0 psum.7
  978.6 0.6 copy.86
  979.2 3.2 all-to-all-start.3
  982.5 0.0 collective-permute-done.1
  982.5 15.4 %bitcast_convert_fusion = bf16[4,768,1024]{2,1,0:T(8,128)(2,1)} fusion(bf16[4,4,320,1024]{3,2,0,1:T(8,128)(2,1)} %bitcast.70, bf16[2,4,320,768]{3,2,1,0:T(8,128)(2,1)} %collective-permute-done.1, bf16[2,4,320,768]{3,2,1,0:T(8,128)(2,1)} %maximum_select_fusion.2, f32[4,4,320]{2,1,0:T(4,128)S(1)} %copy.78, pred[]{:T(512)S(6)} %eq.41), kind=kOutput, calls=%fused_computation.5 | convolution fusion | flops 8079802368 | bytes 24662016 | tf_op jit(solution)/shard_map/nerf,enrd->efd/dot_general | solution.py:72
  998.0 0.0 all-to-all-done.3
  998.0 0.1 reshape.202
  998.0 6.2 gather_fusion.1
  1004.2 0.1 reshape.214
  1004.3 0.7 copy.93
  (25 shorter events, 0.3 us)
Async XLA Ops:
  9.4 73.1 %all-to-all-start.1 = ((bf16[128,4,1024]{2,0,1:T(8,128)(2,1)}), bf16[128,4,1024]{2,0,1:T(8,128)(2,1)S(1)}, u32[]{:S(2)}, u32[]{:S(2)}) async-start(bf16[128,4,1024]{2,0,1:T(8,128)(2,1)} %bitcast.62), calls=%async_computation.1 | async-start | bytes 2097152 | tf_op jit(solution)/shard_map/all_to_all | solution.py:28
  15.8 953.1 %all-reduce.3.cloned.1.call-start = ((), (), s32[]{:S(2)}) async-start(), calls=%async_computation.4 | async-start | bytes 31457280
  257.1 1.5 copy-start
  258.6 147.5 %copy-start.2 = (bf16[128,8]{0,1:T(8,128)(2,1)S(1)}, bf16[128,8]{0,1:T(8,128)(2,1)}, u32[]{:S(2)}) copy-start(bf16[128,8]{0,1:T(8,128)(2,1)} %param.7) | copy-start | bytes 6148
  258.6 518.0 %copy-start.1 = (s32[128,8]{0,1:T(8,128)S(1)}, s32[128,8]{0,1:T(8,128)}, u32[]{:S(2)}) copy-start(s32[128,8]{0,1:T(8,128)} %param.6) | copy-start | bytes 12292
  258.6 518.5 %copy-start.3 = (u32[32]{0:T(128)S(1)}, u32[32]{0:T(128)}, u32[]{:S(2)}) copy-start(u32[32]{0:T(128)} %constant.82) | copy-start | bytes 388
  258.6 142.8 %collective-permute-start = (bf16[1,4,320,768]{3,2,1,0:T(8,128)(2,1)S(1)}, bf16[1,4,320,768]{3,2,1,0:T(8,128)(2,1)}, u32[]{:S(2)}, u32[]{:S(2)}) collective-permute-start(bf16[1,4,320,768]{3,2,1,0:T(8,128)(2,1)S(1)} %copy-done), channel_id=1, source_target_pairs={{0,8},{8,0},{16,24},{24,16},{1,9},{9,1},{17,25},{25,17},{2,10},{10... | collective-permute-start | bytes 5898248 | tf_op jit(solution)/shard_map/ppermute | solution.py:11
  405.7 576.8 %collective-permute-start.1 = (bf16[2,4,320,768]{3,2,1,0:T(8,128)(2,1)}, bf16[2,4,320,768]{3,2,1,0:T(8,128)(2,1)}, u32[]{:S(2)}, u32[]{:S(2)}) collective-permute-start(bf16[2,4,320,768]{3,2,1,0:T(8,128)(2,1)} %maximum_select_fusion.2), channel_id=1, source_target_pairs={{0,16},{8,24},{16,0},{24,8},{1,17},{9,25},{17,1},{25,9},{2,18},{10... | collective-permute-start | bytes 11796488 | tf_op jit(solution)/shard_map/ppermute | solution.py:11
  773.4 7.1 all-to-all-start
  979.2 18.7 %all-to-all-start.3 = ((f32[4,4,80]{2,0,1:T(4,128)}), f32[4,4,80]{2,0,1:T(4,128)S(1)}, u32[]{:S(2)}, u32[]{:S(2)}) async-start(f32[4,4,80]{2,0,1:T(4,128)} %copy.86), calls=%async_computation.3 | async-start | bytes 16384 | tf_op jit(solution)/shard_map/all_to_all | solution.py:88
Sparse Core Ops, SparseCore 0:
  257.2 711.6 all-reduce.2
